TPU v7x, 512 devices: a whole 4x4x16 slice. The times are simulated.
512 devices in a mesh: cluster: 128 (over z, y, x_lo), feat: 4 (over x_hi, core).
Axes of the slice: x: 4 (x_hi: 2, x_lo: 2; x = x_hi * 2 + x_lo), y: 4, z: 16, core: 2. Of those that a mesh axis runs over, the one named last changes fastest.
Arguments:
- queries: bfloat16 [32768, 1024], P('cluster', 'feat'), may hold values from -6 to 6
- assign: int32 [32768, 1], P('cluster'), may hold values from 0 to 127, as said below
- band_mask: int32 [128, 7], replicated, may hold values from 0 to 1, as said below
- keys: bfloat16 [65536, 1024], P(('cluster', 'feat')), may hold values from -6 to 6
- labels: bfloat16 [65536, 1000], P(('cluster', 'feat')), may hold values from -24 to 24
- prior: bfloat16 [65536], P(('cluster', 'feat')), may hold values from -2 to 506
Outputs:
- propagated: bfloat16 [32768, 1000], P('cluster', 'feat')
Inputs may be any that keep to these rules, and one draw needn't show every extreme that they name: `assign`: in each aligned block of 256 rows at most 4 rows name one cluster. `band_mask`: entry 3 of every row is 1.
All inputs are finite; a program needn't handle non-finite values.
Results may differ from a plain program's by a relative error of at most 0.014.
Values may be sent and summed in bfloat16 or wider, within the bound.
No kernel may reach another device: no remote copies, remote signals or barrier semaphores. Data moves between devices by JAX's collectives and lax.ppermute only.
A program may use at most 64 MiB of HBM per device.

v0:
```python
import math
import jax
import jax.numpy as jnp
from jax import lax
from jax.sharding import Mesh
from jax.sharding import PartitionSpec as P

REACH = 3
temper = 2.0
CLUSTER = ("outer", "inner")


def routed(array, forward):
    outer = lax.axis_size("outer")
    inner = lax.axis_size("inner")
    tail = array.shape[1:]
    grid = array.reshape((outer, inner) + tail)
    stages = ("inner", "outer") if forward else ("outer", "inner")
    for axis in stages:
        if axis == "inner":
            grid = jnp.swapaxes(grid, 0, 1)
        grid = lax.all_to_all(grid, axis, split_axis=0, concat_axis=0, tiled=True)
        if axis == "inner":
            grid = jnp.swapaxes(grid, 0, 1)
    return grid.reshape(array.shape)


def shifted(array, axis, by):
    peers = lax.axis_size(axis)
    return lax.ppermute(array, axis, [(i, (i - by) % peers) for i in range(peers)])


def swapped(array, axis, bit):
    peers = lax.axis_size(axis)
    return lax.ppermute(array, axis, [(i, i ^ bit) for i in range(peers)])


def round_bf16(x):
    return lax.reduce_precision(x, exponent_bits=8, mantissa_bits=7)


def split3(x):
    hi = round_bf16(x)
    rest = x - hi
    mid = round_bf16(rest)
    lo = rest - mid
    return [part.astype(jnp.bfloat16) for part in (hi, mid, lo)]


def join3(parts):
    hi, mid, lo = [p.astype(jnp.float32) for p in parts]
    return hi + mid + lo


def pack(part, top, total, width):
    rows = part.shape[0]
    codes = split3(top) + split3(total)
    columns = [part.astype(jnp.bfloat16)] + [c[:, None] for c in codes]
    pad = width - part.shape[1] - len(codes)
    columns.append(jnp.zeros((rows, pad), jnp.bfloat16))
    return jnp.concatenate(columns, axis=1)


def merge(kept, top, total, message, width):
    other = message[:, :width].astype(jnp.float32)
    codes = [message[:, width + i] for i in range(6)]
    other_top = join3(codes[:3])
    other_total = join3(codes[3:])
    highest = jnp.maximum(top, other_top)
    mine = jnp.exp(top - highest)
    theirs = jnp.exp(other_top - highest)
    merged = kept * mine[:, None] + other * theirs[:, None]
    return (merged, highest, total * mine + other_total * theirs)


def body(queries, assign, band_mask, keys, labels, prior):
    clusters = lax.axis_size(CLUSTER)
    cluster_index = lax.axis_index(CLUSTER)
    feat_index = lax.axis_index("feat")
    local_rows = queries.shape[0]
    depth = keys.shape[1]
    classes = labels.shape[1]
    rows = keys.shape[0]
    capacity = 2 * local_rows // clusters
    slots = clusters * capacity
    width = depth + classes + 1
    padded = -(-width // 128) * 128
    block = jnp.concatenate(
        [keys, labels, prior[:, None], jnp.zeros((rows, padded - width), keys.dtype)], axis=1
    )
    offsets = [0]
    for reach in range(1, REACH + 1):
        offsets += [reach, -reach]
    blocks = [block] + [shifted(block, CLUSTER, o) for o in offsets[1:]]
    target = assign[:, 0]
    onehot = (target[:, None] == jnp.arange(clusters, dtype=jnp.int32)[None, :]).astype(jnp.int32)
    before = jnp.cumsum(onehot, axis=0) - onehot
    position = target * capacity + jnp.sum(before * onehot, axis=1)
    outgoing = jnp.zeros((slots, queries.shape[1]), queries.dtype).at[position].set(queries)
    arrived = routed(outgoing.reshape(clusters, capacity, queries.shape[1]), True)
    query_full = lax.all_gather(
        arrived.reshape(slots, queries.shape[1]), "feat", axis=1, tiled=True
    )
    stacked = jnp.stack(blocks)
    band_keys = stacked[:, :, :depth].reshape(len(offsets) * rows, depth)
    band_labels = stacked[:, :, depth : depth + classes].reshape(len(offsets) * rows, classes)
    band_prior = stacked[:, :, depth + classes].reshape(len(offsets) * rows)
    mask_row = band_mask[cluster_index]
    live_blocks = jnp.stack([mask_row[REACH + o] > 0 for o in offsets])
    live = jnp.repeat(live_blocks, rows)
    scale = temper / math.sqrt(depth)
    scores = (
        jnp.einsum("qd,kd->qk", query_full, band_keys, preferred_element_type=jnp.float32) * scale
    )
    scores = scores + band_prior.astype(jnp.float32)[None, :]
    scores = jnp.where(live[None, :], scores, -jnp.inf)
    top = jnp.max(scores, axis=1)
    weight = jnp.exp(scores - top[:, None])
    total = jnp.sum(weight, axis=1)
    accum = jnp.dot(weight.astype(jnp.bfloat16), band_labels, preferred_element_type=jnp.float32)
    quarter = classes // 4
    core = feat_index % 2
    side = feat_index // 2
    grid = accum.reshape(slots, 2, 2, quarter)
    kept = lax.dynamic_index_in_dim(grid, core, axis=2, keepdims=False)
    sent = lax.dynamic_index_in_dim(grid, 1 - core, axis=2, keepdims=False)
    message = swapped(
        pack(sent.reshape(slots, 2 * quarter), top, total, 2 * quarter + 12), "feat", 1
    )
    kept, top, total = merge(kept.reshape(slots, 2 * quarter), top, total, message, 2 * quarter)
    grid = kept.reshape(slots, 2, quarter)
    kept = lax.dynamic_index_in_dim(grid, side, axis=1, keepdims=False)
    sent = lax.dynamic_index_in_dim(grid, 1 - side, axis=1, keepdims=False)
    message = swapped(pack(sent, top, total, quarter + 6), "feat", 2)
    kept, top, total = merge(kept, top, total, message, quarter)
    shares = (kept / total[:, None]).astype(jnp.bfloat16)
    returned = routed(shares.reshape(clusters, capacity, quarter), False)
    return returned.reshape(slots, quarter)[position]


def solution(mesh):
    clusters = mesh.shape["cluster"]
    inner = 8 if clusters % 8 == 0 else 1
    split = Mesh(
        mesh.devices.reshape(clusters // inner, inner, mesh.shape["feat"]),
        ("outer", "inner", "feat"),
    )
    in_specs = (
        P(CLUSTER, "feat"),
        P(CLUSTER, None),
        P(),
        P(CLUSTER + ("feat",), None),
        P(CLUSTER + ("feat",), None),
        P(CLUSTER + ("feat",)),
    )
    out_specs = P(CLUSTER, "feat")
    return jax.shard_map(body, mesh=split, in_specs=in_specs, out_specs=out_specs, check_vma=False)
```

profile of v0, /device:TPU:64, one launch (start us, length us, event | category | flops | bytes accessed | tf_op | source)
XLA Modules:
  0.0 194.4 jit_solution(8708139541104495941)
XLA Ops:
  9.6 5.4 %collective-permute-start = (bf16[128,2048]{1,0:T(8,128)(2,1)S(1)}, bf16[128,2048]{1,0:T(8,128)(2,1)}, u32[]{:S(2)}, u32[]{:S(2)}) collective-permute-start(bf16[128,2048]{1,0:T(8,128)(2,1)S(1)} %concatenate.9), channel_id=1, source_target_pairs={{0,508},{4,0},{8,4},{12,8},{16,12},{20,16},{24,20},{28,24},{32,28}... | collective-permute-start | bytes 1572872 | tf_op jit(solution)/shard_map/ppermute | solution.py:30
  15.0 1.9 collective-permute-start.1
  16.9 3.0 %collective-permute-start.2 = (bf16[128,2048]{1,0:T(8,128)(2,1)S(1)}, bf16[128,2048]{1,0:T(8,128)(2,1)S(1)}, u32[]{:S(2)}, u32[]{:S(2)}) collective-permute-start(bf16[128,2048]{1,0:T(8,128)(2,1)S(1)} %concatenate.9), channel_id=1, source_target_pairs={{0,504},{4,508},{8,0},{12,4},{16,8},{20,12},{24,16},{28,20},{32,24... | collective-permute-start | bytes 1572872 | tf_op jit(solution)/shard_map/ppermute | solution.py:30
  19.9 2.8 %collective-permute-start.3 = (bf16[128,2048]{1,0:T(8,128)(2,1)S(1)}, bf16[128,2048]{1,0:T(8,128)(2,1)S(1)}, u32[]{:S(2)}, u32[]{:S(2)}) collective-permute-start(bf16[128,2048]{1,0:T(8,128)(2,1)S(1)} %concatenate.9), channel_id=1, source_target_pairs={{0,8},{4,12},{8,16},{12,20},{16,24},{20,28},{24,32},{28,36},{32,40... | collective-permute-start | bytes 1572872 | tf_op jit(solution)/shard_map/ppermute | solution.py:30
  22.8 6.4 %collective-permute-start.4 = (bf16[128,2048]{1,0:T(8,128)(2,1)S(1)}, bf16[128,2048]{1,0:T(8,128)(2,1)S(1)}, u32[]{:S(2)}, u32[]{:S(2)}) collective-permute-start(bf16[128,2048]{1,0:T(8,128)(2,1)S(1)} %concatenate.9), channel_id=1, source_target_pairs={{0,500},{4,504},{8,508},{12,0},{16,4},{20,8},{24,12},{28,16},{32,2... | collective-permute-start | bytes 1572872 | tf_op jit(solution)/shard_map/ppermute | solution.py:30
  30.5 1.9 scatter_custom_fusion
  33.3 4.8 %all-to-all-start = ((bf16[8,16,4,256]{3,2,1,0:T(4,128)(2,1)}), bf16[8,16,4,256]{3,2,1,0:T(4,128)(2,1)S(1)}, u32[]{:S(2)}, u32[]{:S(2)}) async-start(bf16[8,16,4,256]{3,2,1,0:T(4,128)(2,1)} %bitcast.80), calls=%async_computation | async-start | bytes 524288 | tf_op jit(solution)/shard_map/all_to_all | solution.py:22
  44.0 8.9 %all-to-all-done = bf16[8,16,4,256]{3,2,1,0:T(4,128)(2,1)S(1)} async-done(((bf16[8,16,4,256]{3,2,1,0:T(4,128)(2,1)}), bf16[8,16,4,256]{3,2,1,0:T(4,128)(2,1)S(1)}, u32[]{:S(2)}, u32[]{:S(2)}) %all-to-all-start) | async-done | bytes 262176 | tf_op jit(solution)/shard_map/all_to_all | solution.py:22
  53.8 14.9 %all-to-all-start.1 = ((bf16[16,8,4,256]{3,2,1,0:T(4,128)(2,1)}), bf16[16,8,4,256]{3,2,1,0:T(4,128)(2,1)S(1)}, u32[]{:S(2)}, u32[]{:S(2)}) async-start(bf16[16,8,4,256]{3,2,1,0:T(4,128)(2,1)} %copy.50), calls=%async_computation.1 | async-start | bytes 524288 | tf_op jit(solution)/shard_map/all_to_all | solution.py:22
  68.8 11.5 %collective-permute-start.5 = (bf16[128,2048]{1,0:T(8,128)(2,1)S(1)}, bf16[128,2048]{1,0:T(8,128)(2,1)}, u32[]{:S(2)}, u32[]{:S(2)}) collective-permute-start(bf16[128,2048]{1,0:T(8,128)(2,1)S(1)} %concatenate.9), channel_id=1, source_target_pairs={{0,12},{4,16},{8,20},{12,24},{16,28},{20,32},{24,36},{28,40},{32,4... | collective-permute-start | bytes 1572872 | tf_op jit(solution)/shard_map/ppermute | solution.py:30
  80.3 1.9 bitcast_dynamic-update-slice_fusion.5
  83.0 3.7 %all-to-all-done.1 = bf16[16,8,4,256]{3,2,1,0:T(4,128)(2,1)S(1)} async-done(((bf16[16,8,4,256]{3,2,1,0:T(4,128)(2,1)}), bf16[16,8,4,256]{3,2,1,0:T(4,128)(2,1)S(1)}, u32[]{:S(2)}, u32[]{:S(2)}) %all-to-all-start.1) | async-done | bytes 262176 | tf_op jit(solution)/shard_map/all_to_all | solution.py:22
  90.1 11.3 %collective-permute-done.5 = bf16[128,2048]{1,0:T(8,128)(2,1)} collective-permute-done((bf16[128,2048]{1,0:T(8,128)(2,1)S(1)}, bf16[128,2048]{1,0:T(8,128)(2,1)}, u32[]{:S(2)}, u32[]{:S(2)}) %collective-permute-start.5) | collective-permute-done | bytes 524320 | tf_op jit(solution)/shard_map/ppermute | solution.py:30
  101.3 1.9 bitcast_dynamic-update-slice_fusion
  103.2 1.8 slice.116
  107.3 3.0 %reshape.184 = bf16[2,2,250,896]{2,1,0,3:T(2,128)(2,1)} reshape(bf16[1000,896]{0,1:T(8,128)(2,1)S(1)} %bitcast.84) | data formatting | bytes 3584000 | tf_op jit(solution)/shard_map/dot_general | solution.py:120
  111.4 6.3 %all-gather.2.cloned.1.call-done = bf16[512,1024]{1,0:T(8,128)(2,1)} async-done(((bf16[512,256]{1,0:T(8,128)(2,1)}), bf16[512,1024]{1,0:T(8,128)(2,1)}) %all-gather.2.cloned.1.call-update) | async-done | bytes 1048592 | tf_op jit(solution)/shard_map/all_gather | solution.py:101
  117.7 3.2 %fusion.40 = (f32[512]{0:T(512)S(1)}, f32[512,896]{1,0:T(8,128)S(1)}) fusion(f32[896]{0:T(1024)S(1)} %bitcast.103, bf16[512,1024]{1,0:T(8,128)(2,1)} %all-gather.2.cloned.1.call-done, bf16[896,1024]{1,0:T(8,128)(2,1)} %bitcast.85, pred[896]{0:T(1024)(128)(4,1)S(1)} %broadcast_bitcast_fusion), kind=kOutput, calls=%fused_computation.95 | convolution fusion | flops 941358592 | bytes 4725120 | tf_op jit(solution)/shard_map/qd,kd->qk/dot_general | solution.py:113
  125.7 2.2 %collective-permute-start.6 = (bf16[512,512]{0,1:T(8,128)(2,1)S(1)}, bf16[512,512]{0,1:T(8,128)(2,1)S(1)}, u32[]{:S(2)}, u32[]{:S(2)}) collective-permute-start(bf16[512,512]{0,1:T(8,128)(2,1)S(1)} %concatenate.10), channel_id=1, source_target_pairs={{0,1},{1,0},{2,3},{3,2},{4,5},{5,4},{6,7},{7,6},{8,9},{9,8},{10,11... | collective-permute-start | bytes 1572872 | tf_op jit(solution)/shard_map/ppermute | solution.py:35
  130.1 2.5 %collective-permute-start.7 = (bf16[512,256]{0,1:T(8,128)(2,1)S(1)}, bf16[512,256]{0,1:T(8,128)(2,1)S(1)}, u32[]{:S(2)}, u32[]{:S(2)}) collective-permute-start(bf16[512,256]{0,1:T(8,128)(2,1)S(1)} %concatenate.11), channel_id=1, source_target_pairs={{0,2},{1,3},{2,0},{3,1},{4,6},{5,7},{6,4},{7,5},{8,10},{9,11},{10,... | collective-permute-start | bytes 786440 | tf_op jit(solution)/shard_map/ppermute | solution.py:35
  132.6 9.4 %collective-permute-done.7 = bf16[512,256]{0,1:T(8,128)(2,1)S(1)} collective-permute-done((bf16[512,256]{0,1:T(8,128)(2,1)S(1)}, bf16[512,256]{0,1:T(8,128)(2,1)S(1)}, u32[]{:S(2)}, u32[]{:S(2)}) %collective-permute-start.7) | collective-permute-done | bytes 262176 | tf_op jit(solution)/shard_map/ppermute | solution.py:35
  142.3 30.7 %all_to_all.20 = bf16[16,8,4,250]{3,2,1,0:T(4,128)(2,1)S(1)} all-to-all(bf16[16,8,4,250]{3,2,1,0:T(4,128)(2,1)S(1)} %reshape_reshape.14), channel_id=1, replica_groups=mesh['outer'=16,'inner'=8,'feat'=4] {'outer'}, dimensions={0} | all-to-all | bytes 512000 | tf_op jit(solution)/shard_map/all_to_all | solution.py:22
  173.8 4.3 %all-to-all-start.3 = ((bf16[8,16,4,250]{3,2,1,0:T(4,128)(2,1)}), bf16[8,16,4,250]{3,2,1,0:T(4,128)(2,1)S(1)}, u32[]{:S(2)}, u32[]{:S(2)}) async-start(bf16[8,16,4,250]{3,2,1,0:T(4,128)(2,1)} %copy.55), calls=%async_computation.3 | async-start | bytes 524288 | tf_op jit(solution)/shard_map/all_to_all | solution.py:22
  178.1 7.3 %all-to-all-done.3 = bf16[8,16,4,250]{3,2,1,0:T(4,128)(2,1)S(1)} async-done(((bf16[8,16,4,250]{3,2,1,0:T(4,128)(2,1)}), bf16[8,16,4,250]{3,2,1,0:T(4,128)(2,1)S(1)}, u32[]{:S(2)}, u32[]{:S(2)}) %all-to-all-start.3) | async-done | bytes 256032 | tf_op jit(solution)/shard_map/all_to_all | solution.py:22
  (72 shorter events, 25.4 us)
Async XLA Ops:
  6.5 32.4 %copy-start = (s32[128,7]{0,1:T(8,128)S(1)}, s32[128,7]{0,1:T(8,128)}, u32[]{:S(2)}) copy-start(s32[128,7]{0,1:T(8,128)} %param.8) | copy-start | bytes 10756
  6.5 23.7 %copy-start.4 = (s32[256,1]{0,1:T(1,128)S(1)}, s32[256,1]{0,1:T(1,128)}, u32[]{:S(2)}) copy-start(s32[256,1]{0,1:T(1,128)} %param.7) | copy-start | bytes 3076
  9.6 59.2 %collective-permute-start = (bf16[128,2048]{1,0:T(8,128)(2,1)S(1)}, bf16[128,2048]{1,0:T(8,128)(2,1)}, u32[]{:S(2)}, u32[]{:S(2)}) collective-permute-start(bf16[128,2048]{1,0:T(8,128)(2,1)S(1)} %concatenate.9), channel_id=1, source_target_pairs={{0,508},{4,0},{8,4},{12,8},{16,12},{20,16},{24,20},{28,24},{32,28}... | collective-permute-start | bytes 1572872 | tf_op jit(solution)/shard_map/ppermute | solution.py:30
  15.0 67.1 %collective-permute-start.1 = (bf16[128,2048]{1,0:T(8,128)(2,1)S(1)}, bf16[128,2048]{1,0:T(8,128)(2,1)S(1)}, u32[]{:S(2)}, u32[]{:S(2)}) collective-permute-start(bf16[128,2048]{1,0:T(8,128)(2,1)S(1)} %concatenate.9), channel_id=1, source_target_pairs={{0,4},{4,8},{8,12},{12,16},{16,20},{20,24},{24,28},{28,32},{32,36}... | collective-permute-start | bytes 1572872 | tf_op jit(solution)/shard_map/ppermute | solution.py:30
  16.9 70.6 %collective-permute-start.2 = (bf16[128,2048]{1,0:T(8,128)(2,1)S(1)}, bf16[128,2048]{1,0:T(8,128)(2,1)S(1)}, u32[]{:S(2)}, u32[]{:S(2)}) collective-permute-start(bf16[128,2048]{1,0:T(8,128)(2,1)S(1)} %concatenate.9), channel_id=1, source_target_pairs={{0,504},{4,508},{8,0},{12,4},{16,8},{20,12},{24,16},{28,20},{32,24... | collective-permute-start | bytes 1572872 | tf_op jit(solution)/shard_map/ppermute | solution.py:30
  19.9 68.4 %collective-permute-start.3 = (bf16[128,2048]{1,0:T(8,128)(2,1)S(1)}, bf16[128,2048]{1,0:T(8,128)(2,1)S(1)}, u32[]{:S(2)}, u32[]{:S(2)}) collective-permute-start(bf16[128,2048]{1,0:T(8,128)(2,1)S(1)} %concatenate.9), channel_id=1, source_target_pairs={{0,8},{4,12},{8,16},{12,20},{16,24},{20,28},{24,32},{28,36},{32,40... | collective-permute-start | bytes 1572872 | tf_op jit(solution)/shard_map/ppermute | solution.py:30
  22.8 66.4 %collective-permute-start.4 = (bf16[128,2048]{1,0:T(8,128)(2,1)S(1)}, bf16[128,2048]{1,0:T(8,128)(2,1)S(1)}, u32[]{:S(2)}, u32[]{:S(2)}) collective-permute-start(bf16[128,2048]{1,0:T(8,128)(2,1)S(1)} %concatenate.9), channel_id=1, source_target_pairs={{0,500},{4,504},{8,508},{12,0},{16,4},{20,8},{24,12},{28,16},{32,2... | collective-permute-start | bytes 1572872 | tf_op jit(solution)/shard_map/ppermute | solution.py:30
  33.3 19.7 %all-to-all-start = ((bf16[8,16,4,256]{3,2,1,0:T(4,128)(2,1)}), bf16[8,16,4,256]{3,2,1,0:T(4,128)(2,1)S(1)}, u32[]{:S(2)}, u32[]{:S(2)}) async-start(bf16[8,16,4,256]{3,2,1,0:T(4,128)(2,1)} %bitcast.80), calls=%async_computation | async-start | bytes 524288 | tf_op jit(solution)/shard_map/all_to_all | solution.py:22
  53.8 33.0 %all-to-all-start.1 = ((bf16[16,8,4,256]{3,2,1,0:T(4,128)(2,1)}), bf16[16,8,4,256]{3,2,1,0:T(4,128)(2,1)S(1)}, u32[]{:S(2)}, u32[]{:S(2)}) async-start(bf16[16,8,4,256]{3,2,1,0:T(4,128)(2,1)} %copy.50), calls=%async_computation.1 | async-start | bytes 524288 | tf_op jit(solution)/shard_map/all_to_all | solution.py:22
  68.7 49.0 %all-gather.2.cloned.1.call-start = ((), (), s32[]{:S(2)}) async-start(), calls=%async_computation.4 | async-start | bytes 1310720 | tf_op jit(solution)/shard_map/all_gather | solution.py:101
  68.8 32.6 %collective-permute-start.5 = (bf16[128,2048]{1,0:T(8,128)(2,1)S(1)}, bf16[128,2048]{1,0:T(8,128)(2,1)}, u32[]{:S(2)}, u32[]{:S(2)}) collective-permute-start(bf16[128,2048]{1,0:T(8,128)(2,1)S(1)} %concatenate.9), channel_id=1, source_target_pairs={{0,12},{4,16},{8,20},{12,24},{16,28},{20,32},{24,36},{28,40},{32,4... | collective-permute-start | bytes 1572872 | tf_op jit(solution)/shard_map/ppermute | solution.py:30
  103.2 2.6 %copy-start.1 = (bf16[7,128,2048]{2,1,0:T(8,128)(2,1)S(1)}, bf16[7,128,2048]{2,1,0:T(8,128)(2,1)}, u32[]{:S(2)}) copy-start(bf16[7,128,2048]{2,1,0:T(8,128)(2,1)} %bitcast_dynamic-update-slice_fusion) | copy-start | bytes 11010052
  120.9 1.5 copy-start.2
  123.8 1.3 copy-start.3
  125.7 3.8 %collective-permute-start.6 = (bf16[512,512]{0,1:T(8,128)(2,1)S(1)}, bf16[512,512]{0,1:T(8,128)(2,1)S(1)}, u32[]{:S(2)}, u32[]{:S(2)}) collective-permute-start(bf16[512,512]{0,1:T(8,128)(2,1)S(1)} %concatenate.10), channel_id=1, source_target_pairs={{0,1},{1,0},{2,3},{3,2},{4,5},{5,4},{6,7},{7,6},{8,9},{9,8},{10,11... | collective-permute-start | bytes 1572872 | tf_op jit(solution)/shard_map/ppermute | solution.py:35
  130.1 11.9 %collective-permute-start.7 = (bf16[512,256]{0,1:T(8,128)(2,1)S(1)}, bf16[512,256]{0,1:T(8,128)(2,1)S(1)}, u32[]{:S(2)}, u32[]{:S(2)}) collective-permute-start(bf16[512,256]{0,1:T(8,128)(2,1)S(1)} %concatenate.11), channel_id=1, source_target_pairs={{0,2},{1,3},{2,0},{3,1},{4,6},{5,7},{6,4},{7,5},{8,10},{9,11},{10,... | collective-permute-start | bytes 786440 | tf_op jit(solution)/shard_map/ppermute | solution.py:35
  173.8 11.6 %all-to-all-start.3 = ((bf16[8,16,4,250]{3,2,1,0:T(4,128)(2,1)}), bf16[8,16,4,250]{3,2,1,0:T(4,128)(2,1)S(1)}, u32[]{:S(2)}, u32[]{:S(2)}) async-start(bf16[8,16,4,250]{3,2,1,0:T(4,128)(2,1)} %copy.55), calls=%async_computation.3 | async-start | bytes 524288 | tf_op jit(solution)/shard_map/all_to_all | solution.py:22
Sparse Core Ops, SparseCore 0:
  87.7 29.9 all-gather.1
where the time goes:
time: 195 us; the launch traced here: 194 us
  starting transfers between devices  59.6 us (31%)
  waiting for transfers between devices  47.1 us (24%)
  local copies, waits for them, and re-layouts  31.7 us (16%)
  blocking collectives  30.7 us (16%)
  between operations  18.1 us (9%)
  matrix products  4.64 us (2%)
  other arithmetic  2.49 us (1%)
    ppermute x6, starting transfers between devices, shifted(): lax.ppermute(array, axis, [(i, (i - by) % peers) for i in range(peers)])  31 us
    all_to_all x1, blocking collectives, routed(): grid = lax.all_to_all(grid, axis, split_axis=0, concat_axis=0, tiled=True)  30.7 us
    all_to_all x3, starting transfers between devices, routed(): grid = lax.all_to_all(grid, axis, split_axis=0, concat_axis=0, tiled=True)  24 us
    all_to_all x3, waiting for transfers between devices, routed(): grid = lax.all_to_all(grid, axis, split_axis=0, concat_axis=0, tiled=True)  19.9 us
    ppermute x6, waiting for transfers between devices, shifted(): lax.ppermute(array, axis, [(i, (i - by) % peers) for i in range(peers)])  11.3 us
    unnamed x18, local copies, waits for them, and re-layouts  10.4 us
    ppermute x2, waiting for transfers between devices, swapped(): return lax.ppermute(array, axis, [(i, i ^ bit) for i in range(peers)])  9.58 us
    all_gather x1, waiting for transfers between devices, body(): lax.all_gather(arrived.reshape(slots, queries.shape[1]), 'feat', axis=1,...  6.28 us
  transfers between devices with their start and end apart: 12, of which 7 were waited for; matrix products, arithmetic and copies ran while one was open for 12% of the time, Pallas kernels for 0%

commit v1 on v0

--- a/solution.py
+++ b/solution.py
@@ -98,8 +98,14 @@
     position = target * capacity + jnp.sum(before * onehot, axis=1)
     outgoing = jnp.zeros((slots, queries.shape[1]), queries.dtype).at[position].set(queries)
     arrived = routed(outgoing.reshape(clusters, capacity, queries.shape[1]), True)
-    query_full = lax.all_gather(
-        arrived.reshape(slots, queries.shape[1]), "feat", axis=1, tiled=True
+    query_full = jnp.concatenate(
+        lax.all_to_all(
+            jnp.stack([arrived.reshape(slots, queries.shape[1])] * lax.axis_size("feat")),
+            "feat",
+            0,
+            0,
+        ),
+        axis=1,
     )
     stacked = jnp.stack(blocks)
     band_keys = stacked[:, :, :depth].reshape(len(offsets) * rows, depth)

time: 195 us -> 175 us (0.90)
  between operations: 18.1 us -> 4.76 us
  waiting for transfers between devices: 47.1 us -> 34 us
  starting transfers between devices: 59.6 us -> 65.6 us
    all_gather x1 -> x0, waiting for transfers between devices: 6.28 us -> none  [body(): lax.all_gather(arrived.reshape(slots, queries.shape[1]), 'feat', axis=1,...]
    all_to_all x0 -> x1, starting transfers between devices: none -> 4.47 us  [body(): lax.all_to_all(jnp.stack([arrived.reshape(slots, queries.shape[1])] * lax...]
    ppermute x6, waiting for transfers between devices: 11.3 us -> 8.01 us  [shifted(): lax.ppermute(array, axis, [(i, (i - by) % peers) for i in range(peers)])]
  transfers between devices with their start and end apart: 12 -> 12, of which waited for: 7 -> 6; matrix products, arithmetic and copies ran while one was open for 12% -> 14% of each run, Pallas kernels for 0% -> 0%
where the time goes in v1:
time: 175 us; the launch traced here: 174 us
  starting transfers between devices  65.6 us (37%)
  waiting for transfers between devices  34 us (19%)
  local copies, waits for them, and re-layouts  32.2 us (18%)
  blocking collectives  30.4 us (17%)
  between operations  4.76 us (3%)
  matrix products  4.35 us (2%)
  other arithmetic  2.49 us (1%)
    ppermute x6, starting transfers between devices, shifted(): lax.ppermute(array, axis, [(i, (i - by) % peers) for i in range(peers)])  31 us
    all_to_all x1, blocking collectives, routed(): grid = lax.all_to_all(grid, axis, split_axis=0, concat_axis=0, tiled=True)  30.4 us
    all_to_all x3, starting transfers between devices, routed(): grid = lax.all_to_all(grid, axis, split_axis=0, concat_axis=0, tiled=True)  23.8 us
    all_to_all x3, waiting for transfers between devices, routed(): grid = lax.all_to_all(grid, axis, split_axis=0, concat_axis=0, tiled=True)  18.2 us
    unnamed x18, local copies, waits for them, and re-layouts  10.3 us
    ppermute x6, waiting for transfers between devices, shifted(): lax.ppermute(array, axis, [(i, (i - by) % peers) for i in range(peers)])  8.01 us
    ppermute x2, waiting for transfers between devices, swapped(): return lax.ppermute(array, axis, [(i, i ^ bit) for i in range(peers)])  7.78 us
    ppermute x2, starting transfers between devices, swapped(): return lax.ppermute(array, axis, [(i, i ^ bit) for i in range(peers)])  6.3 us
  transfers between devices with their start and end apart: 12, of which 6 were waited for; matrix products, arithmetic and copies ran while one was open for 14% of the time, Pallas kernels for 0%

profile of v1, /device:TPU:64, one launch (start us, length us, event | category | flops | bytes accessed | tf_op | source)
XLA Modules:
  0.0 173.8 jit_solution(5428680603433696129)
XLA Ops:
  3.1 5.4 %collective-permute-start = (bf16[128,2048]{1,0:T(8,128)(2,1)S(1)}, bf16[128,2048]{1,0:T(8,128)(2,1)}, u32[]{:S(2)}, u32[]{:S(2)}) collective-permute-start(bf16[128,2048]{1,0:T(8,128)(2,1)S(1)} %concatenate.9), channel_id=1, source_target_pairs={{0,508},{4,0},{8,4},{12,8},{16,12},{20,16},{24,20},{28,24},{32,28}... | collective-permute-start | bytes 1572872 | tf_op jit(solution)/shard_map/ppermute | solution.py:30
  8.5 1.9 %collective-permute-start.1 = (bf16[128,2048]{1,0:T(8,128)(2,1)S(1)}, bf16[128,2048]{1,0:T(8,128)(2,1)S(1)}, u32[]{:S(2)}, u32[]{:S(2)}) collective-permute-start(bf16[128,2048]{1,0:T(8,128)(2,1)S(1)} %concatenate.9), channel_id=1, source_target_pairs={{0,4},{4,8},{8,12},{12,16},{16,20},{20,24},{24,28},{28,32},{32,36}... | collective-permute-start | bytes 1572872 | tf_op jit(solution)/shard_map/ppermute | solution.py:30
  10.4 3.0 %collective-permute-start.2 = (bf16[128,2048]{1,0:T(8,128)(2,1)S(1)}, bf16[128,2048]{1,0:T(8,128)(2,1)S(1)}, u32[]{:S(2)}, u32[]{:S(2)}) collective-permute-start(bf16[128,2048]{1,0:T(8,128)(2,1)S(1)} %concatenate.9), channel_id=1, source_target_pairs={{0,504},{4,508},{8,0},{12,4},{16,8},{20,12},{24,16},{28,20},{32,24... | collective-permute-start | bytes 1572872 | tf_op jit(solution)/shard_map/ppermute | solution.py:30
  13.4 2.8 %collective-permute-start.3 = (bf16[128,2048]{1,0:T(8,128)(2,1)S(1)}, bf16[128,2048]{1,0:T(8,128)(2,1)S(1)}, u32[]{:S(2)}, u32[]{:S(2)}) collective-permute-start(bf16[128,2048]{1,0:T(8,128)(2,1)S(1)} %concatenate.9), channel_id=1, source_target_pairs={{0,8},{4,12},{8,16},{12,20},{16,24},{20,28},{24,32},{28,36},{32,40... | collective-permute-start | bytes 1572872 | tf_op jit(solution)/shard_map/ppermute | solution.py:30
  16.3 6.4 %collective-permute-start.4 = (bf16[128,2048]{1,0:T(8,128)(2,1)S(1)}, bf16[128,2048]{1,0:T(8,128)(2,1)S(1)}, u32[]{:S(2)}, u32[]{:S(2)}) collective-permute-start(bf16[128,2048]{1,0:T(8,128)(2,1)S(1)} %concatenate.9), channel_id=1, source_target_pairs={{0,500},{4,504},{8,508},{12,0},{16,4},{20,8},{24,12},{28,16},{32,2... | collective-permute-start | bytes 1572872 | tf_op jit(solution)/shard_map/ppermute | solution.py:30
  23.9 1.9 %scatter_custom_fusion = bf16[512,256]{1,0:T(8,128)(2,1)S(1)} fusion(s32[256]{0:T(256)S(1)} %bitcast.109, bf16[256,256]{1,0:T(8,128)(2,1)} %param.6, bf16[]{:T(256)} %constant.76.clone.1), kind=kCustom, calls=%fused_computation.34 | custom fusion | bytes 262656 | tf_op jit(solution)/shard_map/scatter | solution.py:99
  26.7 4.8 %all-to-all-start = ((bf16[8,16,4,256]{3,2,1,0:T(4,128)(2,1)}), bf16[8,16,4,256]{3,2,1,0:T(4,128)(2,1)S(1)}, u32[]{:S(2)}, u32[]{:S(2)}) async-start(bf16[8,16,4,256]{3,2,1,0:T(4,128)(2,1)} %bitcast.83), calls=%async_computation | async-start | bytes 524288 | tf_op jit(solution)/shard_map/all_to_all | solution.py:22
  37.6 8.8 %all-to-all-done = bf16[8,16,4,256]{3,2,1,0:T(4,128)(2,1)S(1)} async-done(((bf16[8,16,4,256]{3,2,1,0:T(4,128)(2,1)}), bf16[8,16,4,256]{3,2,1,0:T(4,128)(2,1)S(1)}, u32[]{:S(2)}, u32[]{:S(2)}) %all-to-all-start) | async-done | bytes 262176 | tf_op jit(solution)/shard_map/all_to_all | solution.py:22
  47.2 14.9 %all-to-all-start.1 = ((bf16[16,8,4,256]{3,2,1,0:T(4,128)(2,1)}), bf16[16,8,4,256]{3,2,1,0:T(4,128)(2,1)S(1)}, u32[]{:S(2)}, u32[]{:S(2)}) async-start(bf16[16,8,4,256]{3,2,1,0:T(4,128)(2,1)} %copy.53), calls=%async_computation.1 | async-start | bytes 524288 | tf_op jit(solution)/shard_map/all_to_all | solution.py:22
  62.1 11.5 %collective-permute-start.5 = (bf16[128,2048]{1,0:T(8,128)(2,1)S(1)}, bf16[128,2048]{1,0:T(8,128)(2,1)}, u32[]{:S(2)}, u32[]{:S(2)}) collective-permute-start(bf16[128,2048]{1,0:T(8,128)(2,1)S(1)} %concatenate.9), channel_id=1, source_target_pairs={{0,12},{4,16},{8,20},{12,24},{16,28},{20,32},{24,36},{28,40},{32,4... | collective-permute-start | bytes 1572872 | tf_op jit(solution)/shard_map/ppermute | solution.py:30
  73.6 1.9 %bitcast_dynamic-update-slice_fusion.5 = bf16[7,128,2048]{2,1,0:T(8,128)(2,1)} fusion(bf16[7,128,2048]{2,1,0:T(8,128)(2,1)} %bitcast_dynamic-update-slice_fusion.6, bf16[128,2048]{1,0:T(8,128)(2,1)} %collective-permute-done), kind=kLoop, calls=%fused_computation.21 | loop fusion | bytes 1048576
  78.1 2.1 %all-to-all-done.1 = bf16[16,8,4,256]{3,2,1,0:T(4,128)(2,1)S(1)} async-done(((bf16[16,8,4,256]{3,2,1,0:T(4,128)(2,1)}), bf16[16,8,4,256]{3,2,1,0:T(4,128)(2,1)S(1)}, u32[]{:S(2)}, u32[]{:S(2)}) %all-to-all-start.1) | async-done | bytes 262176 | tf_op jit(solution)/shard_map/all_to_all | solution.py:22
  81.5 4.5 %all-to-all-start.2 = ((bf16[4,512,256]{1,2,0:T(8,128)(2,1)}), bf16[4,512,256]{1,2,0:T(8,128)(2,1)S(1)}, u32[]{:S(2)}, u32[]{:S(2)}) async-start(bf16[4,512,256]{1,2,0:T(8,128)(2,1)} %stack.59), calls=%async_computation.2 | async-start | bytes 2097152 | tf_op jit(solution)/shard_map/all_to_all | solution.py:102
  86.8 8.0 %collective-permute-done.5 = bf16[128,2048]{1,0:T(8,128)(2,1)} collective-permute-done((bf16[128,2048]{1,0:T(8,128)(2,1)S(1)}, bf16[128,2048]{1,0:T(8,128)(2,1)}, u32[]{:S(2)}, u32[]{:S(2)}) %collective-permute-start.5) | collective-permute-done | bytes 524320 | tf_op jit(solution)/shard_map/ppermute | solution.py:30
  94.8 1.9 %bitcast_dynamic-update-slice_fusion = bf16[7,128,2048]{2,1,0:T(8,128)(2,1)} fusion(bf16[7,128,2048]{2,1,0:T(8,128)(2,1)} %bitcast_dynamic-update-slice_fusion.1, bf16[128,2048]{1,0:T(8,128)(2,1)} %collective-permute-done.5), kind=kLoop, calls=%fused_computation.16 | loop fusion | bytes 1048576 | tf_op jit(solution)/shard_map/stack | solution.py:110
  96.7 1.8 %slice.116 = bf16[7,128,1000]{2,1,0:T(8,128)(2,1)S(1)} slice(bf16[7,128,2048]{2,1,0:T(8,128)(2,1)} %bitcast_dynamic-update-slice_fusion), slice={[0:7], [0:128], [1024:2024]} | slice | bytes 3584000 | tf_op jit(solution)/shard_map/slice | solution.py:112
  100.7 3.0 %reshape.194 = bf16[2,2,250,896]{2,1,0,3:T(2,128)(2,1)} reshape(bf16[1000,896]{0,1:T(8,128)(2,1)S(1)} %bitcast.87) | data formatting | bytes 3584000 | tf_op jit(solution)/shard_map/dot_general | solution.py:126
  104.9 2.9 %fusion.40 = (f32[512]{0:T(512)S(1)}, f32[512,896]{1,0:T(8,128)S(1)}) fusion(f32[896]{0:T(1024)S(1)} %bitcast.107, bf16[512,1024]{0,1:T(8,128)(2,1)S(1)} %bitcast.89, bf16[896,1024]{1,0:T(8,128)(2,1)} %bitcast.88, pred[896]{0:T(1024)(128)(4,1)S(1)} %broadcast_bitcast_fusion), kind=kOutput, calls=%fused_computation.95 | convolution fusion | flops 941358592 | bytes 4725120 | tf_op jit(solution)/shard_map/qd,kd->qk/dot_general | solution.py:119
  112.7 1.9 %collective-permute-start.6 = (bf16[512,512]{0,1:T(8,128)(2,1)S(1)}, bf16[512,512]{0,1:T(8,128)(2,1)S(1)}, u32[]{:S(2)}, u32[]{:S(2)}) collective-permute-start(bf16[512,512]{0,1:T(8,128)(2,1)S(1)} %concatenate.10), channel_id=1, source_target_pairs={{0,1},{1,0},{2,3},{3,2},{4,5},{5,4},{6,7},{7,6},{8,9},{9,8},{10,11... | collective-permute-start | bytes 1572872 | tf_op jit(solution)/shard_map/ppermute | solution.py:35
  117.0 4.4 %collective-permute-start.7 = (bf16[512,256]{0,1:T(8,128)(2,1)S(1)}, bf16[512,256]{0,1:T(8,128)(2,1)S(1)}, u32[]{:S(2)}, u32[]{:S(2)}) collective-permute-start(bf16[512,256]{0,1:T(8,128)(2,1)S(1)} %concatenate.11), channel_id=1, source_target_pairs={{0,2},{1,3},{2,0},{3,1},{4,6},{5,7},{6,4},{7,5},{8,10},{9,11},{10,... | collective-permute-start | bytes 786440 | tf_op jit(solution)/shard_map/ppermute | solution.py:35
  121.4 7.3 %collective-permute-done.7 = bf16[512,256]{0,1:T(8,128)(2,1)S(1)} collective-permute-done((bf16[512,256]{0,1:T(8,128)(2,1)S(1)}, bf16[512,256]{0,1:T(8,128)(2,1)S(1)}, u32[]{:S(2)}, u32[]{:S(2)}) %collective-permute-start.7) | collective-permute-done | bytes 262176 | tf_op jit(solution)/shard_map/ppermute | solution.py:35
  129.1 30.4 %all_to_all.25 = bf16[16,8,4,250]{3,2,1,0:T(4,128)(2,1)S(1)} all-to-all(bf16[16,8,4,250]{3,2,1,0:T(4,128)(2,1)S(1)} %reshape_reshape.10), channel_id=1, replica_groups=mesh['outer'=16,'inner'=8,'feat'=4] {'outer'}, dimensions={0} | all-to-all | bytes 512000 | tf_op jit(solution)/shard_map/all_to_all | solution.py:22
  160.3 4.1 %all-to-all-start.4 = ((bf16[8,16,4,250]{3,2,1,0:T(4,128)(2,1)}), bf16[8,16,4,250]{3,2,1,0:T(4,128)(2,1)S(1)}, u32[]{:S(2)}, u32[]{:S(2)}) async-start(bf16[8,16,4,250]{3,2,1,0:T(4,128)(2,1)} %copy.59), calls=%async_computation.4 | async-start | bytes 524288 | tf_op jit(solution)/shard_map/all_to_all | solution.py:22
  164.5 7.3 %all-to-all-done.4 = bf16[8,16,4,250]{3,2,1,0:T(4,128)(2,1)S(1)} async-done(((bf16[8,16,4,250]{3,2,1,0:T(4,128)(2,1)}), bf16[8,16,4,250]{3,2,1,0:T(4,128)(2,1)S(1)}, u32[]{:S(2)}, u32[]{:S(2)}) %all-to-all-start.4) | async-done | bytes 256032 | tf_op jit(solution)/shard_map/all_to_all | solution.py:22
  (73 shorter events, 26.1 us)
Async XLA Ops:
  0.0 32.4 %copy-start = (s32[128,7]{0,1:T(8,128)S(1)}, s32[128,7]{0,1:T(8,128)}, u32[]{:S(2)}) copy-start(s32[128,7]{0,1:T(8,128)} %param.8) | copy-start | bytes 10756
  0.0 23.7 %copy-start.4 = (s32[256,1]{0,1:T(1,128)S(1)}, s32[256,1]{0,1:T(1,128)}, u32[]{:S(2)}) copy-start(s32[256,1]{0,1:T(1,128)} %param.7) | copy-start | bytes 3076
  3.1 59.1 %collective-permute-start = (bf16[128,2048]{1,0:T(8,128)(2,1)S(1)}, bf16[128,2048]{1,0:T(8,128)(2,1)}, u32[]{:S(2)}, u32[]{:S(2)}) collective-permute-start(bf16[128,2048]{1,0:T(8,128)(2,1)S(1)} %concatenate.9), channel_id=1, source_target_pairs={{0,508},{4,0},{8,4},{12,8},{16,12},{20,16},{24,20},{28,24},{32,28}... | collective-permute-start | bytes 1572872 | tf_op jit(solution)/shard_map/ppermute | solution.py:30
  8.5 67.1 %collective-permute-start.1 = (bf16[128,2048]{1,0:T(8,128)(2,1)S(1)}, bf16[128,2048]{1,0:T(8,128)(2,1)S(1)}, u32[]{:S(2)}, u32[]{:S(2)}) collective-permute-start(bf16[128,2048]{1,0:T(8,128)(2,1)S(1)} %concatenate.9), channel_id=1, source_target_pairs={{0,4},{4,8},{8,12},{12,16},{16,20},{20,24},{24,28},{28,32},{32,36}... | collective-permute-start | bytes 1572872 | tf_op jit(solution)/shard_map/ppermute | solution.py:30
  10.4 66.0 %collective-permute-start.2 = (bf16[128,2048]{1,0:T(8,128)(2,1)S(1)}, bf16[128,2048]{1,0:T(8,128)(2,1)S(1)}, u32[]{:S(2)}, u32[]{:S(2)}) collective-permute-start(bf16[128,2048]{1,0:T(8,128)(2,1)S(1)} %concatenate.9), channel_id=1, source_target_pairs={{0,504},{4,508},{8,0},{12,4},{16,8},{20,12},{24,16},{28,20},{32,24... | collective-permute-start | bytes 1572872 | tf_op jit(solution)/shard_map/ppermute | solution.py:30
  13.4 63.8 %collective-permute-start.3 = (bf16[128,2048]{1,0:T(8,128)(2,1)S(1)}, bf16[128,2048]{1,0:T(8,128)(2,1)S(1)}, u32[]{:S(2)}, u32[]{:S(2)}) collective-permute-start(bf16[128,2048]{1,0:T(8,128)(2,1)S(1)} %concatenate.9), channel_id=1, source_target_pairs={{0,8},{4,12},{8,16},{12,20},{16,24},{20,28},{24,32},{28,36},{32,40... | collective-permute-start | bytes 1572872 | tf_op jit(solution)/shard_map/ppermute | solution.py:30
  16.3 69.7 %collective-permute-start.4 = (bf16[128,2048]{1,0:T(8,128)(2,1)S(1)}, bf16[128,2048]{1,0:T(8,128)(2,1)S(1)}, u32[]{:S(2)}, u32[]{:S(2)}) collective-permute-start(bf16[128,2048]{1,0:T(8,128)(2,1)S(1)} %concatenate.9), channel_id=1, source_target_pairs={{0,500},{4,504},{8,508},{12,0},{16,4},{20,8},{24,12},{28,16},{32,2... | collective-permute-start | bytes 1572872 | tf_op jit(solution)/shard_map/ppermute | solution.py:30
  26.7 19.7 %all-to-all-start = ((bf16[8,16,4,256]{3,2,1,0:T(4,128)(2,1)}), bf16[8,16,4,256]{3,2,1,0:T(4,128)(2,1)S(1)}, u32[]{:S(2)}, u32[]{:S(2)}) async-start(bf16[8,16,4,256]{3,2,1,0:T(4,128)(2,1)} %bitcast.83), calls=%async_computation | async-start | bytes 524288 | tf_op jit(solution)/shard_map/all_to_all | solution.py:22
  47.2 33.0 %all-to-all-start.1 = ((bf16[16,8,4,256]{3,2,1,0:T(4,128)(2,1)}), bf16[16,8,4,256]{3,2,1,0:T(4,128)(2,1)S(1)}, u32[]{:S(2)}, u32[]{:S(2)}) async-start(bf16[16,8,4,256]{3,2,1,0:T(4,128)(2,1)} %copy.53), calls=%async_computation.1 | async-start | bytes 524288 | tf_op jit(solution)/shard_map/all_to_all | solution.py:22
  62.1 32.7 %collective-permute-start.5 = (bf16[128,2048]{1,0:T(8,128)(2,1)S(1)}, bf16[128,2048]{1,0:T(8,128)(2,1)}, u32[]{:S(2)}, u32[]{:S(2)}) collective-permute-start(bf16[128,2048]{1,0:T(8,128)(2,1)S(1)} %concatenate.9), channel_id=1, source_target_pairs={{0,12},{4,16},{8,20},{12,24},{16,28},{20,32},{24,36},{28,40},{32,4... | collective-permute-start | bytes 1572872 | tf_op jit(solution)/shard_map/ppermute | solution.py:30
  81.5 23.4 %all-to-all-start.2 = ((bf16[4,512,256]{1,2,0:T(8,128)(2,1)}), bf16[4,512,256]{1,2,0:T(8,128)(2,1)S(1)}, u32[]{:S(2)}, u32[]{:S(2)}) async-start(bf16[4,512,256]{1,2,0:T(8,128)(2,1)} %stack.59), calls=%async_computation.2 | async-start | bytes 2097152 | tf_op jit(solution)/shard_map/all_to_all | solution.py:102
  96.7 2.6 %copy-start.1 = (bf16[7,128,2048]{2,1,0:T(8,128)(2,1)S(1)}, bf16[7,128,2048]{2,1,0:T(8,128)(2,1)}, u32[]{:S(2)}) copy-start(bf16[7,128,2048]{2,1,0:T(8,128)(2,1)} %bitcast_dynamic-update-slice_fusion) | copy-start | bytes 11010052
  107.8 1.5 copy-start.2
  110.7 1.3 copy-start.3
  112.7 3.8 %collective-permute-start.6 = (bf16[512,512]{0,1:T(8,128)(2,1)S(1)}, bf16[512,512]{0,1:T(8,128)(2,1)S(1)}, u32[]{:S(2)}, u32[]{:S(2)}) collective-permute-start(bf16[512,512]{0,1:T(8,128)(2,1)S(1)} %concatenate.10), channel_id=1, source_target_pairs={{0,1},{1,0},{2,3},{3,2},{4,5},{5,4},{6,7},{7,6},{8,9},{9,8},{10,11... | collective-permute-start | bytes 1572872 | tf_op jit(solution)/shard_map/ppermute | solution.py:35
  117.0 11.7 %collective-permute-start.7 = (bf16[512,256]{0,1:T(8,128)(2,1)S(1)}, bf16[512,256]{0,1:T(8,128)(2,1)S(1)}, u32[]{:S(2)}, u32[]{:S(2)}) collective-permute-start(bf16[512,256]{0,1:T(8,128)(2,1)S(1)} %concatenate.11), channel_id=1, source_target_pairs={{0,2},{1,3},{2,0},{3,1},{4,6},{5,7},{6,4},{7,5},{8,10},{9,11},{10,... | collective-permute-start | bytes 786440 | tf_op jit(solution)/shard_map/ppermute | solution.py:35
  160.3 11.4 %all-to-all-start.4 = ((bf16[8,16,4,250]{3,2,1,0:T(4,128)(2,1)}), bf16[8,16,4,250]{3,2,1,0:T(4,128)(2,1)S(1)}, u32[]{:S(2)}, u32[]{:S(2)}) async-start(bf16[8,16,4,250]{3,2,1,0:T(4,128)(2,1)} %copy.59), calls=%async_computation.4 | async-start | bytes 524288 | tf_op jit(solution)/shard_map/all_to_all | solution.py:22
